TPU v7x, 256 devices: a whole 4x4x8 slice. The times are simulated.
256 devices in a mesh: pos: 16 (over x_hi, z), exp: 16 (over y, x_lo, core).
Axes of the slice: x: 4 (x_hi: 2, x_lo: 2; x = x_hi * 2 + x_lo), y: 4, z: 8, core: 2. Of those that a mesh axis runs over, the one named last changes fastest.
Arguments:
- patches: bfloat16 [65536, 4, 256], P(('pos', 'exp')), may hold values from -6 to 6
- conv_weight: bfloat16 [3, 256, 2048], replicated, may hold values from -0.21875 to 0.21875
- phi: bfloat16 [2048, 128], replicated, may hold values from -40 to 40, as said below
- w_in: bfloat16 [16, 2048, 8192], P('exp', None, 'pos'), may hold values from -0.125 to 0.125
- w_out: bfloat16 [16, 8192, 2048], P('exp', 'pos'), may hold values from -0.0625 to 0.0625
Outputs:
- mixed: bfloat16 [65536, 4, 2048], P(('pos', 'exp'))
Inputs may be any that keep to these rules, and one draw needn't show every extreme that they name: phi is real-valued.
All inputs are finite; a program needn't handle non-finite values.
Results may differ from a plain program's by a relative error of at most 0.019.
The roundings to bfloat16 on the way count: a program that leaves them out, or rounds other values in their place, can miss the bound.
Values may be sent and summed in bfloat16 or wider, within the bound.
No kernel may reach another device: no remote copies, remote signals or barrier semaphores. Data moves between devices by JAX's collectives and lax.ppermute only.
A program may use at most 128 MiB of HBM per device.

v0:
```python
import jax
import jax.numpy as jnp
from jax import lax
from jax.sharding import PartitionSpec as P

D = 2048
SLOTS_PER = 8


def with_halo(array, sides, width):
    for axis, dim in sides:
        count, length = (lax.axis_size(axis), array.shape[dim])
        up = [(i, (i + 1) % count) for i in range(count - 1)]
        down = [(j, i) for i, j in up]
        last = lax.slice_in_dim(array, length - width, length, axis=dim)
        initial = lax.slice_in_dim(array, 0, width, axis=dim)
        before = lax.ppermute(last, axis, up)
        after = lax.ppermute(initial, axis, down)
        array = jnp.concatenate([before, array, after], axis=dim)
    return array


def butterfly_sum(value, axis):
    count = lax.axis_size(axis)
    step = 1
    while step < count:
        pairs = [(i, i ^ step) for i in range(count)]
        value = value + lax.ppermute(value, axis, pairs)
        step *= 2
    return value


def gather_rows(row, axes):
    count = lax.axis_size(axes)
    tiled = jnp.broadcast_to(row[None, :], (count, row.shape[0]))
    return lax.all_to_all(tiled, axes, 0, 0, tiled=True)


def per_device(patches, conv_weight, phi, w_in, w_out):
    channels, periods, samples = patches.shape
    every = ("pos", "exp")
    padded = with_halo(patches, ((every, 0),), 1)
    running = jnp.zeros((channels * periods, D), jnp.float32)
    for offset in range(3):
        window = padded[offset : offset + channels].reshape(channels * periods, samples)
        running = running + jnp.dot(window, conv_weight[offset], preferred_element_type=jnp.float32)
    flat = running.astype(jnp.bfloat16)
    logits = jnp.dot(flat, phi, preferred_element_type=jnp.float32)
    slots = logits.shape[1]
    local_peak = jnp.max(logits, axis=0)
    local_total = jnp.sum(jnp.exp(logits - local_peak), axis=0)
    stats = gather_rows(jnp.concatenate([local_peak, local_total]), every)
    peaks, totals = (stats[:, :slots], stats[:, slots:])
    column_peak = jnp.max(peaks, axis=0)
    column_total = jnp.sum(totals * jnp.exp(peaks - column_peak), axis=0)
    raw_weights = jnp.exp(logits - column_peak)
    dispatch = (raw_weights / column_total).astype(jnp.bfloat16)
    every_slot = lax.dot_general(
        dispatch, flat, (((0,), (0,)), ((), ())), preferred_element_type=jnp.float32
    )
    groups = lax.axis_size("exp")
    mine = lax.all_to_all(every_slot, "exp", 0, 0, tiled=True)
    owned = jnp.sum(mine.reshape(groups, SLOTS_PER, D), axis=0)
    slot_in = butterfly_sum(owned, "pos").astype(jnp.bfloat16)
    hidden = jax.nn.gelu(
        jnp.dot(slot_in, w_in[0], preferred_element_type=jnp.float32), approximate=True
    ).astype(jnp.bfloat16)
    expert_term = jnp.dot(hidden, w_out[0], preferred_element_type=jnp.float32)
    slot_out = butterfly_sum(expert_term, "pos").astype(jnp.bfloat16)
    row_peak = jnp.max(logits, axis=1, keepdims=True)
    row_weights = jnp.exp(logits - row_peak)
    combine = (row_weights / jnp.sum(row_weights, axis=1, keepdims=True)).astype(jnp.bfloat16)
    mixed = jnp.dot(
        combine,
        lax.all_gather(slot_out, "exp", axis=0, tiled=True),
        preferred_element_type=jnp.float32,
    )
    return mixed.astype(jnp.bfloat16).reshape(channels, periods, D)


def solution(mesh):
    in_specs = (
        P(("pos", "exp"), None, None),
        P(),
        P(),
        P("exp", None, "pos"),
        P("exp", "pos", None),
    )
    out_specs = P(("pos", "exp"), None, None)
    return jax.shard_map(
        per_device, mesh=mesh, in_specs=in_specs, out_specs=out_specs, check_vma=False
    )
```

profile of v0, /device:TPU:1, one launch (start us, length us, event | category | flops | bytes accessed | tf_op | source)
XLA Modules:
  0.0 161.6 jit_solution(5333478168599324480)
XLA Ops:
  0.0 0.0 copy-start
  0.0 0.9 fusion.44
  0.9 5.1 %collective-permute-start.1 = (bf16[1,4,256]{2,1,0:T(4,128)(2,1)S(1)}, bf16[1,4,256]{2,1,0:T(4,128)(2,1)S(1)}, u32[]{:S(2)}, u32[]{:S(2)}) collective-permute-start(bf16[1,4,256]{2,1,0:T(4,128)(2,1)S(1)} %get-tuple-element.11), channel_id=1, source_target_pairs={{1,0},{2,1},{3,2},{4,3},{5,4},{6,5},{7,6},{8,7},{9,8},{10,9},{11,1... | collective-permute-start | bytes 6152 | tf_op jit(solution)/shard_map/ppermute | solution.py:18
  6.0 1.9 %collective-permute-start = (bf16[1,4,256]{2,1,0:T(4,128)(2,1)S(1)}, bf16[1,4,256]{2,1,0:T(4,128)(2,1)S(1)}, u32[]{:S(2)}, u32[]{:S(2)}) collective-permute-start(bf16[1,4,256]{2,1,0:T(4,128)(2,1)S(1)} %get-tuple-element.12), channel_id=1, source_target_pairs={{0,1},{1,2},{2,3},{3,4},{4,5},{5,6},{6,7},{7,8},{8,9},{9,10},{10,1... | collective-permute-start | bytes 6152 | tf_op jit(solution)/shard_map/ppermute | solution.py:17
  7.9 1.2 reshape.28
  9.1 0.0 copy-start.2
  9.1 5.8 %fusion.8 = f32[1024,2048]{1,0:T(8,128)} fusion(bf16[1024,256]{1,0:T(8,128)(2,1)S(1)} %reshape.28, bf16[3,256,2048]{2,1,0:T(8,128)(2,1)} %param.6), kind=kOutput, calls=%fused_computation.9 | convolution fusion | flops 1073741824 | bytes 9961472 | tf_op jit(solution)/shard_map/dot_general | solution.py:46
  14.8 0.0 collective-permute-done.1
  14.8 0.0 collective-permute-done
  14.8 0.0 copy-done.2
  14.8 1.2 pad_maximum_fusion
  16.0 0.1 reshape.29
  16.1 1.2 reshape.27
  17.3 0.0 copy-start.1
  17.3 2.6 %fusion.10 = f32[1024,2048]{1,0:T(8,128)S(1)} fusion(bf16[1024,256]{1,0:T(8,128)(2,1)S(1)} %reshape.27, bf16[3,256,2048]{2,1,0:T(8,128)(2,1)} %param.6), kind=kOutput, calls=%fused_computation.11 | convolution fusion | flops 1073741824 | bytes 9961472 | tf_op jit(solution)/shard_map/dot_general | solution.py:46
  20.0 1.0 copy-done.1
  21.0 0.0 copy-start.3
  21.0 2.7 %add_convert_fusion = bf16[1024,2048]{1,0:T(8,128)(2,1)S(1)} fusion(f32[1024,2048]{1,0:T(8,128)S(1)} %fusion.10, f32[1024,2048]{1,0:T(8,128)S(1)} %copy-done.1, bf16[1024,256]{1,0:T(8,128)(2,1)S(1)} %reshape.29, bf16[3,256,2048]{2,1,0:T(8,128)(2,1)} %param.6), kind=kOutput, calls=%fused_computation | convolution fusion | flops 1080033280 | bytes 22544384 | tf_op jit(solution)/shard_map/dot_general | solution.py:46
  23.7 0.0 copy-done.3
  23.8 1.3 fusion.43
  25.1 0.4 fusion.15
  25.5 0.1 broadcast_in_dim.2
  25.6 31.6 %all_to_all.18 = f32[256,1,256]{2,1,0:T(1,128)S(1)} all-to-all(f32[256,1,256]{2,1,0:T(1,128)S(1)} %broadcast_in_dim.2), channel_id=1, replica_groups=mesh['pos'=16,'exp'=16] {'pos','exp'}, dimensions={0} | all-to-all | bytes 524288 | tf_op jit(solution)/shard_map/all_to_all | solution.py:36
  57.3 0.1 fusion.20
  57.4 0.8 convolution_bitcast_fusion
  58.2 18.9 %all_to_all.19 = f32[16,8,2048]{2,1,0:T(8,128)} all-to-all(f32[16,8,2048]{2,1,0:T(8,128)S(1)} %convolution_bitcast_fusion), channel_id=1, replica_groups=mesh['pos'=16,'exp'=16] {'exp'}, dimensions={0} | all-to-all | bytes 2097152 | tf_op jit(solution)/shard_map/all_to_all | solution.py:62
  77.1 1.3 reduce_sum.39
  78.4 0.9 collective-permute-start.2
  79.2 2.3 %collective-permute-done.2 = f32[8,2048]{1,0:T(8,128)S(1)} collective-permute-done((f32[8,2048]{1,0:T(8,128)S(1)}, f32[8,2048]{1,0:T(8,128)S(1)}, u32[]{:S(2)}, u32[]{:S(2)}) %collective-permute-start.2) | collective-permute-done | bytes 65568 | tf_op jit(solution)/shard_map/ppermute | solution.py:28
  81.6 0.6 collective-permute-start.3
  82.2 4.2 %collective-permute-done.3 = f32[8,2048]{1,0:T(8,128)S(1)} collective-permute-done((f32[8,2048]{1,0:T(8,128)S(1)}, f32[8,2048]{1,0:T(8,128)S(1)}, u32[]{:S(2)}, u32[]{:S(2)}) %collective-permute-start.3) | collective-permute-done | bytes 65568 | tf_op jit(solution)/shard_map/ppermute | solution.py:28
  86.4 1.1 collective-permute-start.4
  87.5 6.3 %collective-permute-done.4 = f32[8,2048]{1,0:T(8,128)S(1)} collective-permute-done((f32[8,2048]{1,0:T(8,128)S(1)}, f32[8,2048]{1,0:T(8,128)S(1)}, u32[]{:S(2)}, u32[]{:S(2)}) %collective-permute-start.4) | collective-permute-done | bytes 65568 | tf_op jit(solution)/shard_map/ppermute | solution.py:28
  93.7 1.3 collective-permute-start.5
  95.0 3.4 %collective-permute-done.5 = f32[8,2048]{1,0:T(8,128)S(1)} collective-permute-done((f32[8,2048]{1,0:T(8,128)S(1)}, f32[8,2048]{1,0:T(8,128)S(1)}, u32[]{:S(2)}, u32[]{:S(2)}) %collective-permute-start.5) | collective-permute-done | bytes 65568 | tf_op jit(solution)/shard_map/ppermute | solution.py:28
  98.4 0.0 copy-done
  98.4 2.3 %fusion = f32[8,2048]{1,0:T(8,128)S(1)} fusion(bf16[1,512,2048]{2,1,0:T(8,128)(2,1)S(1)} %copy-done, bf16[1,2048,512]{2,1,0:T(8,128)(2,1)} %param.8, f32[8,2048]{1,0:T(8,128)S(1)} %add.43, f32[8,2048]{1,0:T(8,128)S(1)} %collective-permute-done.5), kind=kOutput, calls=%fused_computation.3 | convolution fusion | flops 33624064 | bytes 4390912 | tf_op jit(solution)/shard_map/dot_general | solution.py:68
  100.8 0.2 collective-permute-start.6
  101.0 3.1 %collective-permute-done.6 = f32[8,2048]{1,0:T(8,128)S(1)} collective-permute-done((f32[8,2048]{1,0:T(8,128)S(1)}, f32[8,2048]{1,0:T(8,128)S(1)}, u32[]{:S(2)}, u32[]{:S(2)}) %collective-permute-start.6) | collective-permute-done | bytes 65568 | tf_op jit(solution)/shard_map/ppermute | solution.py:28
  104.1 0.2 collective-permute-start.7
  104.2 4.4 %collective-permute-done.7 = f32[8,2048]{1,0:T(8,128)S(1)} collective-permute-done((f32[8,2048]{1,0:T(8,128)S(1)}, f32[8,2048]{1,0:T(8,128)S(1)}, u32[]{:S(2)}, u32[]{:S(2)}) %collective-permute-start.7) | collective-permute-done | bytes 65568 | tf_op jit(solution)/shard_map/ppermute | solution.py:28
  108.6 1.1 collective-permute-start.8
  109.7 6.6 %collective-permute-done.8 = f32[8,2048]{1,0:T(8,128)S(1)} collective-permute-done((f32[8,2048]{1,0:T(8,128)S(1)}, f32[8,2048]{1,0:T(8,128)S(1)}, u32[]{:S(2)}, u32[]{:S(2)}) %collective-permute-start.8) | collective-permute-done | bytes 65568 | tf_op jit(solution)/shard_map/ppermute | solution.py:28
  116.3 1.2 collective-permute-start.9
  117.5 3.6 %collective-permute-done.9 = f32[8,2048]{1,0:T(8,128)S(1)} collective-permute-done((f32[8,2048]{1,0:T(8,128)S(1)}, f32[8,2048]{1,0:T(8,128)S(1)}, u32[]{:S(2)}, u32[]{:S(2)}) %collective-permute-start.9) | collective-permute-done | bytes 65568 | tf_op jit(solution)/shard_map/ppermute | solution.py:28
  121.0 30.1 %all_gather.3 = bf16[128,2048]{1,0:T(8,128)(2,1)S(1)} all-gather(bf16[8,2048]{1,0:T(8,128)(2,1)S(1)} %add_convert_fusion.1), channel_id=1, replica_groups=mesh['pos'=16,'exp'=16] {'exp'}, dimensions={0}, use_global_device_ids=true | all-gather | bytes 557056 | tf_op jit(solution)/shard_map/all_gather | solution.py:75
  151.2 3.2 %convolution_convert_fusion = bf16[1024,2048]{1,0:T(8,128)(2,1)} fusion(bf16[128,2048]{1,0:T(8,128)(2,1)S(1)} %all_gather.3, f32[1024,128]{1,0:T(8,128)S(1)} %get-tuple-element.13, f32[1024]{0:T(1024)S(1)} %get-tuple-element.5, f32[1024]{0:T(1024)S(1)} %get-tuple-element.7), kind=kOutput, calls=%fused_computation.1 | convolution fusion | flops 539361280 | bytes 5251072 | tf_op jit(solution)/shard_map/dot_general | solution.py:73
  154.4 7.2 %reshape.30 = bf16[256,4,2048]{2,1,0:T(4,128)(2,1)} reshape(bf16[1024,2048]{1,0:T(8,128)(2,1)} %convolution_convert_fusion) | data formatting | bytes 8388608 | tf_op jit(solution)/shard_map/reshape | solution.py:78
  (10 shorter events, 0.1 us)
Async XLA Ops:
  0.0 98.4 %copy-start = (bf16[1,512,2048]{2,1,0:T(8,128)(2,1)S(1)}, bf16[1,512,2048]{2,1,0:T(8,128)(2,1)}, u32[]{:S(2)}) copy-start(bf16[1,512,2048]{2,1,0:T(8,128)(2,1)} %param.9) | copy-start | bytes 6291460
  0.9 14.0 %collective-permute-start.1 = (bf16[1,4,256]{2,1,0:T(4,128)(2,1)S(1)}, bf16[1,4,256]{2,1,0:T(4,128)(2,1)S(1)}, u32[]{:S(2)}, u32[]{:S(2)}) collective-permute-start(bf16[1,4,256]{2,1,0:T(4,128)(2,1)S(1)} %get-tuple-element.11), channel_id=1, source_target_pairs={{1,0},{2,1},{3,2},{4,3},{5,4},{6,5},{7,6},{8,7},{9,8},{10,9},{11,1... | collective-permute-start | bytes 6152 | tf_op jit(solution)/shard_map/ppermute | solution.py:18
  6.0 8.9 %collective-permute-start = (bf16[1,4,256]{2,1,0:T(4,128)(2,1)S(1)}, bf16[1,4,256]{2,1,0:T(4,128)(2,1)S(1)}, u32[]{:S(2)}, u32[]{:S(2)}) collective-permute-start(bf16[1,4,256]{2,1,0:T(4,128)(2,1)S(1)} %get-tuple-element.12), channel_id=1, source_target_pairs={{0,1},{1,2},{2,3},{3,4},{4,5},{5,6},{6,7},{7,8},{8,9},{9,10},{10,1... | collective-permute-start | bytes 6152 | tf_op jit(solution)/shard_map/ppermute | solution.py:17
  9.1 5.8 %copy-start.2 = (bf16[256,4,256]{2,1,0:T(4,128)(2,1)S(1)}, bf16[256,4,256]{2,1,0:T(4,128)(2,1)}, u32[]{:S(2)}) copy-start(bf16[256,4,256]{2,1,0:T(4,128)(2,1)} %param.5) | copy-start | bytes 1572868
  17.3 3.7 %copy-start.1 = (f32[1024,2048]{1,0:T(8,128)S(1)}, f32[1024,2048]{1,0:T(8,128)}, u32[]{:S(2)}) copy-start(f32[1024,2048]{1,0:T(8,128)} %fusion.8) | copy-start | bytes 25165828
  21.0 2.7 %copy-start.3 = (bf16[2048,128]{1,0:T(8,128)(2,1)S(1)}, bf16[2048,128]{1,0:T(8,128)(2,1)}, u32[]{:S(2)}) copy-start(bf16[2048,128]{1,0:T(8,128)(2,1)} %param.7) | copy-start | bytes 1572868
  78.4 3.2 %collective-permute-start.2 = (f32[8,2048]{1,0:T(8,128)S(1)}, f32[8,2048]{1,0:T(8,128)S(1)}, u32[]{:S(2)}, u32[]{:S(2)}) collective-permute-start(f32[8,2048]{1,0:T(8,128)S(1)} %reduce_sum.39), channel_id=1, source_target_pairs={{0,16},{16,0},{32,48},{48,32},{64,80},{80,64},{96,112},{112,96},{1... | collective-permute-start | bytes 196616 | tf_op jit(solution)/shard_map/ppermute | solution.py:28
  81.6 4.8 %collective-permute-start.3 = (f32[8,2048]{1,0:T(8,128)S(1)}, f32[8,2048]{1,0:T(8,128)S(1)}, u32[]{:S(2)}, u32[]{:S(2)}) collective-permute-start(f32[8,2048]{1,0:T(8,128)S(1)} %add.41), channel_id=1, source_target_pairs={{0,32},{16,48},{32,0},{48,16},{64,96},{80,112},{96,64},{112,80},{1... | collective-permute-start | bytes 196616 | tf_op jit(solution)/shard_map/ppermute | solution.py:28
  86.4 7.3 %collective-permute-start.4 = (f32[8,2048]{1,0:T(8,128)S(1)}, f32[8,2048]{1,0:T(8,128)S(1)}, u32[]{:S(2)}, u32[]{:S(2)}) collective-permute-start(f32[8,2048]{1,0:T(8,128)S(1)} %add.42), channel_id=1, source_target_pairs={{0,64},{16,80},{32,96},{48,112},{64,0},{80,16},{96,32},{112,48},{1... | collective-permute-start | bytes 196616 | tf_op jit(solution)/shard_map/ppermute | solution.py:28
  93.7 4.7 %collective-permute-start.5 = (f32[8,2048]{1,0:T(8,128)S(1)}, f32[8,2048]{1,0:T(8,128)S(1)}, u32[]{:S(2)}, u32[]{:S(2)}) collective-permute-start(f32[8,2048]{1,0:T(8,128)S(1)} %add.43), channel_id=1, source_target_pairs={{0,128},{16,144},{32,160},{48,176},{64,192},{80,208},{96,224},{112... | collective-permute-start | bytes 196616 | tf_op jit(solution)/shard_map/ppermute | solution.py:28
  100.8 3.3 %collective-permute-start.6 = (f32[8,2048]{1,0:T(8,128)S(1)}, f32[8,2048]{1,0:T(8,128)S(1)}, u32[]{:S(2)}, u32[]{:S(2)}) collective-permute-start(f32[8,2048]{1,0:T(8,128)S(1)} %fusion), channel_id=1, source_target_pairs={{0,16},{16,0},{32,48},{48,32},{64,80},{80,64},{96,112},{112,96},{1... | collective-permute-start | bytes 196616 | tf_op jit(solution)/shard_map/ppermute | solution.py:28
  104.1 4.5 %collective-permute-start.7 = (f32[8,2048]{1,0:T(8,128)S(1)}, f32[8,2048]{1,0:T(8,128)S(1)}, u32[]{:S(2)}, u32[]{:S(2)}) collective-permute-start(f32[8,2048]{1,0:T(8,128)S(1)} %add.48), channel_id=1, source_target_pairs={{0,32},{16,48},{32,0},{48,16},{64,96},{80,112},{96,64},{112,80},{1... | collective-permute-start | bytes 196616 | tf_op jit(solution)/shard_map/ppermute | solution.py:28
  108.6 7.7 %collective-permute-start.8 = (f32[8,2048]{1,0:T(8,128)S(1)}, f32[8,2048]{1,0:T(8,128)S(1)}, u32[]{:S(2)}, u32[]{:S(2)}) collective-permute-start(f32[8,2048]{1,0:T(8,128)S(1)} %add.49), channel_id=1, source_target_pairs={{0,64},{16,80},{32,96},{48,112},{64,0},{80,16},{96,32},{112,48},{1... | collective-permute-start | bytes 196616 | tf_op jit(solution)/shard_map/ppermute | solution.py:28
  116.3 4.7 %collective-permute-start.9 = (f32[8,2048]{1,0:T(8,128)S(1)}, f32[8,2048]{1,0:T(8,128)S(1)}, u32[]{:S(2)}, u32[]{:S(2)}) collective-permute-start(f32[8,2048]{1,0:T(8,128)S(1)} %add.50), channel_id=1, source_target_pairs={{0,128},{16,144},{32,160},{48,176},{64,192},{80,208},{96,224},{112... | collective-permute-start | bytes 196616 | tf_op jit(solution)/shard_map/ppermute | solution.py:28
where the time goes:
time: 162 us
  blocking collectives  80.7 us (50%)
  waiting for transfers between devices  33.8 us (21%)
  matrix products  18.8 us (12%)
  starting transfers between devices  13.4 us (8%)
  local copies, waits for them, and re-layouts  11.7 us (7%)
  other arithmetic  3 us (2%)
    ppermute x8, waiting for transfers between devices, butterfly_sum(): value = value + lax.ppermute(value, axis, pairs)  33.8 us
    all_to_all x1, blocking collectives, gather_rows(): return lax.all_to_all(tiled, axes, 0, 0, tiled=True)  31.6 us
    all_gather x1, blocking collectives, per_device(): lax.all_gather(slot_out, 'exp', axis=0, tiled=True)  30.1 us
    all_to_all x1, blocking collectives, per_device(): mine = lax.all_to_all(every_slot, 'exp', 0, 0, tiled=True)  18.9 us
    dot_general x3, matrix products, per_device(): jnp.dot(window, conv_weight[offset], preferred_element_type=jnp.float32)  11.1 us
    reshape x1, local copies, waits for them, and re-layouts, per_device(): return mixed.astype(jnp.bfloat16).reshape(channels, periods, D)  7.16 us
    ppermute x8, starting transfers between devices, butterfly_sum(): value = value + lax.ppermute(value, axis, pairs)  6.42 us
    ppermute x1, starting transfers between devices, with_halo(): after = lax.ppermute(initial, axis, down)  5.1 us
  transfers between devices with their start and end apart: 10, of which 8 were waited for; matrix products, arithmetic and copies ran while one was open for 4% of the time, Pallas kernels for 0%

commit v1 on v0

--- a/solution.py
+++ b/solution.py
@@ -72,7 +72,9 @@
     combine = (row_weights / jnp.sum(row_weights, axis=1, keepdims=True)).astype(jnp.bfloat16)
     mixed = jnp.dot(
         combine,
-        lax.all_gather(slot_out, "exp", axis=0, tiled=True),
+        jnp.concatenate(
+            lax.all_to_all(jnp.stack([slot_out] * lax.axis_size("exp")), "exp", 0, 0), axis=0
+        ),
         preferred_element_type=jnp.float32,
     )
     return mixed.astype(jnp.bfloat16).reshape(channels, periods, D)

time: 162 us -> 155 us (0.957)
  blocking collectives: 80.7 us -> 73.4 us
    all_gather x1 -> x0, blocking collectives: 30.1 us -> none  [per_device(): lax.all_gather(slot_out, 'exp', axis=0, tiled=True)]
    all_to_all x0 -> x1, blocking collectives: none -> 22.9 us  [per_device(): lax.all_to_all(jnp.stack([slot_out] * lax.axis_size('exp')), 'exp', 0, 0)]
where the time goes in v1:
time: 155 us; the launch traced here: 154 us
  blocking collectives  73.4 us (47%)
  waiting for transfers between devices  33.8 us (22%)
  matrix products  18.8 us (12%)
  starting transfers between devices  13.4 us (9%)
  local copies, waits for them, and re-layouts  11.7 us (8%)
  other arithmetic  3 us (2%)
    ppermute x8, waiting for transfers between devices, butterfly_sum(): value = value + lax.ppermute(value, axis, pairs)  33.8 us
    all_to_all x1, blocking collectives, gather_rows(): return lax.all_to_all(tiled, axes, 0, 0, tiled=True)  31.6 us
    all_to_all x1, blocking collectives, per_device(): lax.all_to_all(jnp.stack([slot_out] * lax.axis_size('exp')), 'exp', 0, 0)  22.9 us
    all_to_all x1, blocking collectives, per_device(): mine = lax.all_to_all(every_slot, 'exp', 0, 0, tiled=True)  18.9 us
    dot_general x3, matrix products, per_device(): jnp.dot(window, conv_weight[offset], preferred_element_type=jnp.float32)  11.1 us
    reshape x1, local copies, waits for them, and re-layouts, per_device(): return mixed.astype(jnp.bfloat16).reshape(channels, periods, D)  7.16 us
    ppermute x8, starting transfers between devices, butterfly_sum(): value = value + lax.ppermute(value, axis, pairs)  6.42 us
    ppermute x1, starting transfers between devices, with_halo(): after = lax.ppermute(initial, axis, down)  5.1 us
  transfers between devices with their start and end apart: 10, of which 8 were waited for; matrix products, arithmetic and copies ran while one was open for 4% of the time, Pallas kernels for 0%

profile of v1, /device:TPU:1, one launch (start us, length us, event | category | flops | bytes accessed | tf_op | source)
XLA Modules:
  0.0 154.4 jit_solution(15296549741433625101)
XLA Ops:
  0.0 0.0 copy-start
  0.0 0.9 fusion.45
  0.9 5.1 %collective-permute-start.1 = (bf16[1,4,256]{2,1,0:T(4,128)(2,1)S(1)}, bf16[1,4,256]{2,1,0:T(4,128)(2,1)S(1)}, u32[]{:S(2)}, u32[]{:S(2)}) collective-permute-start(bf16[1,4,256]{2,1,0:T(4,128)(2,1)S(1)} %get-tuple-element.11), channel_id=1, source_target_pairs={{1,0},{2,1},{3,2},{4,3},{5,4},{6,5},{7,6},{8,7},{9,8},{10,9},{11,1... | collective-permute-start | bytes 6152 | tf_op jit(solution)/shard_map/ppermute | solution.py:18
  6.0 1.9 %collective-permute-start = (bf16[1,4,256]{2,1,0:T(4,128)(2,1)S(1)}, bf16[1,4,256]{2,1,0:T(4,128)(2,1)S(1)}, u32[]{:S(2)}, u32[]{:S(2)}) collective-permute-start(bf16[1,4,256]{2,1,0:T(4,128)(2,1)S(1)} %get-tuple-element.12), channel_id=1, source_target_pairs={{0,1},{1,2},{2,3},{3,4},{4,5},{5,6},{6,7},{7,8},{8,9},{9,10},{10,1... | collective-permute-start | bytes 6152 | tf_op jit(solution)/shard_map/ppermute | solution.py:17
  7.9 1.2 reshape.33
  9.1 0.0 copy-start.2
  9.1 5.8 %fusion.8 = f32[1024,2048]{1,0:T(8,128)} fusion(bf16[1024,256]{1,0:T(8,128)(2,1)S(1)} %reshape.33, bf16[3,256,2048]{2,1,0:T(8,128)(2,1)} %param.6), kind=kOutput, calls=%fused_computation.9 | convolution fusion | flops 1073741824 | bytes 9961472 | tf_op jit(solution)/shard_map/dot_general | solution.py:46
  14.8 0.0 collective-permute-done.1
  14.8 0.0 collective-permute-done
  14.8 0.0 copy-done.2
  14.8 1.2 pad_maximum_fusion
  16.0 0.1 reshape.34
  16.1 1.2 reshape.32
  17.3 0.0 copy-start.1
  17.3 2.6 %fusion.10 = f32[1024,2048]{1,0:T(8,128)S(1)} fusion(bf16[1024,256]{1,0:T(8,128)(2,1)S(1)} %reshape.32, bf16[3,256,2048]{2,1,0:T(8,128)(2,1)} %param.6), kind=kOutput, calls=%fused_computation.11 | convolution fusion | flops 1073741824 | bytes 9961472 | tf_op jit(solution)/shard_map/dot_general | solution.py:46
  20.0 1.0 copy-done.1
  21.0 0.0 copy-start.3
  21.0 2.7 %add_convert_fusion = bf16[1024,2048]{1,0:T(8,128)(2,1)S(1)} fusion(f32[1024,2048]{1,0:T(8,128)S(1)} %fusion.10, f32[1024,2048]{1,0:T(8,128)S(1)} %copy-done.1, bf16[1024,256]{1,0:T(8,128)(2,1)S(1)} %reshape.34, bf16[3,256,2048]{2,1,0:T(8,128)(2,1)} %param.6), kind=kOutput, calls=%fused_computation | convolution fusion | flops 1080033280 | bytes 22544384 | tf_op jit(solution)/shard_map/dot_general | solution.py:46
  23.7 0.0 copy-done.3
  23.8 1.3 fusion.44
  25.1 0.4 fusion.16
  25.5 0.1 broadcast_in_dim.2
  25.6 31.6 %all_to_all.23 = f32[256,1,256]{2,1,0:T(1,128)S(1)} all-to-all(f32[256,1,256]{2,1,0:T(1,128)S(1)} %broadcast_in_dim.2), channel_id=1, replica_groups=mesh['pos'=16,'exp'=16] {'pos','exp'}, dimensions={0} | all-to-all | bytes 524288 | tf_op jit(solution)/shard_map/all_to_all | solution.py:36
  57.3 0.1 fusion.21
  57.4 0.8 convolution_bitcast_fusion
  58.2 18.9 %all_to_all.24 = f32[16,8,2048]{2,1,0:T(8,128)} all-to-all(f32[16,8,2048]{2,1,0:T(8,128)S(1)} %convolution_bitcast_fusion), channel_id=1, replica_groups=mesh['pos'=16,'exp'=16] {'exp'}, dimensions={0} | all-to-all | bytes 2097152 | tf_op jit(solution)/shard_map/all_to_all | solution.py:62
  77.1 1.3 reduce_sum.39
  78.4 0.9 collective-permute-start.2
  79.2 2.3 %collective-permute-done.2 = f32[8,2048]{1,0:T(8,128)S(1)} collective-permute-done((f32[8,2048]{1,0:T(8,128)S(1)}, f32[8,2048]{1,0:T(8,128)S(1)}, u32[]{:S(2)}, u32[]{:S(2)}) %collective-permute-start.2) | collective-permute-done | bytes 65568 | tf_op jit(solution)/shard_map/ppermute | solution.py:28
  81.6 0.6 collective-permute-start.3
  82.2 4.2 %collective-permute-done.3 = f32[8,2048]{1,0:T(8,128)S(1)} collective-permute-done((f32[8,2048]{1,0:T(8,128)S(1)}, f32[8,2048]{1,0:T(8,128)S(1)}, u32[]{:S(2)}, u32[]{:S(2)}) %collective-permute-start.3) | collective-permute-done | bytes 65568 | tf_op jit(solution)/shard_map/ppermute | solution.py:28
  86.4 1.1 collective-permute-start.4
  87.5 6.3 %collective-permute-done.4 = f32[8,2048]{1,0:T(8,128)S(1)} collective-permute-done((f32[8,2048]{1,0:T(8,128)S(1)}, f32[8,2048]{1,0:T(8,128)S(1)}, u32[]{:S(2)}, u32[]{:S(2)}) %collective-permute-start.4) | collective-permute-done | bytes 65568 | tf_op jit(solution)/shard_map/ppermute | solution.py:28
  93.7 1.3 collective-permute-start.5
  95.0 3.4 %collective-permute-done.5 = f32[8,2048]{1,0:T(8,128)S(1)} collective-permute-done((f32[8,2048]{1,0:T(8,128)S(1)}, f32[8,2048]{1,0:T(8,128)S(1)}, u32[]{:S(2)}, u32[]{:S(2)}) %collective-permute-start.5) | collective-permute-done | bytes 65568 | tf_op jit(solution)/shard_map/ppermute | solution.py:28
  98.4 0.0 copy-done
  98.4 2.3 %fusion = f32[8,2048]{1,0:T(8,128)S(1)} fusion(bf16[1,512,2048]{2,1,0:T(8,128)(2,1)S(1)} %copy-done, bf16[1,2048,512]{2,1,0:T(8,128)(2,1)} %param.8, f32[8,2048]{1,0:T(8,128)S(1)} %add.43, f32[8,2048]{1,0:T(8,128)S(1)} %collective-permute-done.5), kind=kOutput, calls=%fused_computation.3 | convolution fusion | flops 33624064 | bytes 4390912 | tf_op jit(solution)/shard_map/dot_general | solution.py:68
  100.8 0.2 collective-permute-start.6
  101.0 3.1 %collective-permute-done.6 = f32[8,2048]{1,0:T(8,128)S(1)} collective-permute-done((f32[8,2048]{1,0:T(8,128)S(1)}, f32[8,2048]{1,0:T(8,128)S(1)}, u32[]{:S(2)}, u32[]{:S(2)}) %collective-permute-start.6) | collective-permute-done | bytes 65568 | tf_op jit(solution)/shard_map/ppermute | solution.py:28
  104.1 0.2 collective-permute-start.7
  104.2 4.4 %collective-permute-done.7 = f32[8,2048]{1,0:T(8,128)S(1)} collective-permute-done((f32[8,2048]{1,0:T(8,128)S(1)}, f32[8,2048]{1,0:T(8,128)S(1)}, u32[]{:S(2)}, u32[]{:S(2)}) %collective-permute-start.7) | collective-permute-done | bytes 65568 | tf_op jit(solution)/shard_map/ppermute | solution.py:28
  108.6 1.1 collective-permute-start.8
  109.7 6.6 %collective-permute-done.8 = f32[8,2048]{1,0:T(8,128)S(1)} collective-permute-done((f32[8,2048]{1,0:T(8,128)S(1)}, f32[8,2048]{1,0:T(8,128)S(1)}, u32[]{:S(2)}, u32[]{:S(2)}) %collective-permute-start.8) | collective-permute-done | bytes 65568 | tf_op jit(solution)/shard_map/ppermute | solution.py:28
  116.3 1.2 collective-permute-start.9
  117.5 3.6 %collective-permute-done.9 = f32[8,2048]{1,0:T(8,128)S(1)} collective-permute-done((f32[8,2048]{1,0:T(8,128)S(1)}, f32[8,2048]{1,0:T(8,128)S(1)}, u32[]{:S(2)}, u32[]{:S(2)}) %collective-permute-start.9) | collective-permute-done | bytes 65568 | tf_op jit(solution)/shard_map/ppermute | solution.py:28
  121.1 22.9 %all_to_all.25 = bf16[16,8,2048]{2,1,0:T(8,128)(2,1)S(1)} all-to-all(bf16[16,8,2048]{2,1,0:T(8,128)(2,1)S(1)} %stack.2), channel_id=1, replica_groups=mesh['pos'=16,'exp'=16] {'exp'}, dimensions={0} | all-to-all | bytes 1048576 | tf_op jit(solution)/shard_map/all_to_all | solution.py:76
  143.9 3.3 %convolution_convert_fusion = bf16[1024,2048]{1,0:T(8,128)(2,1)} fusion(bf16[16,8,2048]{2,1,0:T(8,128)(2,1)S(1)} %all_to_all.25, f32[1024,128]{1,0:T(8,128)S(1)} %get-tuple-element.13, f32[1024]{0:T(1024)S(1)} %get-tuple-element.5, f32[1024]{0:T(1024)S(1)} %get-tuple-element.7), kind=kOutput, calls=%fused_computation.1 | convolution fusion | flops 539361280 | bytes 5251072 | tf_op jit(solution)/shard_map/dot_general | solution.py:73
  147.2 7.2 %reshape.36 = bf16[256,4,2048]{2,1,0:T(4,128)(2,1)} reshape(bf16[1024,2048]{1,0:T(8,128)(2,1)} %convolution_convert_fusion) | data formatting | bytes 8388608 | tf_op jit(solution)/shard_map/reshape | solution.py:80
  (11 shorter events, 0.2 us)
Async XLA Ops:
  0.0 98.4 %copy-start = (bf16[1,512,2048]{2,1,0:T(8,128)(2,1)S(1)}, bf16[1,512,2048]{2,1,0:T(8,128)(2,1)}, u32[]{:S(2)}) copy-start(bf16[1,512,2048]{2,1,0:T(8,128)(2,1)} %param.9) | copy-start | bytes 6291460
  0.9 14.0 %collective-permute-start.1 = (bf16[1,4,256]{2,1,0:T(4,128)(2,1)S(1)}, bf16[1,4,256]{2,1,0:T(4,128)(2,1)S(1)}, u32[]{:S(2)}, u32[]{:S(2)}) collective-permute-start(bf16[1,4,256]{2,1,0:T(4,128)(2,1)S(1)} %get-tuple-element.11), channel_id=1, source_target_pairs={{1,0},{2,1},{3,2},{4,3},{5,4},{6,5},{7,6},{8,7},{9,8},{10,9},{11,1... | collective-permute-start | bytes 6152 | tf_op jit(solution)/shard_map/ppermute | solution.py:18
  6.0 8.9 %collective-permute-start = (bf16[1,4,256]{2,1,0:T(4,128)(2,1)S(1)}, bf16[1,4,256]{2,1,0:T(4,128)(2,1)S(1)}, u32[]{:S(2)}, u32[]{:S(2)}) collective-permute-start(bf16[1,4,256]{2,1,0:T(4,128)(2,1)S(1)} %get-tuple-element.12), channel_id=1, source_target_pairs={{0,1},{1,2},{2,3},{3,4},{4,5},{5,6},{6,7},{7,8},{8,9},{9,10},{10,1... | collective-permute-start | bytes 6152 | tf_op jit(solution)/shard_map/ppermute | solution.py:17
  9.1 5.8 %copy-start.2 = (bf16[256,4,256]{2,1,0:T(4,128)(2,1)S(1)}, bf16[256,4,256]{2,1,0:T(4,128)(2,1)}, u32[]{:S(2)}) copy-start(bf16[256,4,256]{2,1,0:T(4,128)(2,1)} %param.5) | copy-start | bytes 1572868
  17.3 3.7 %copy-start.1 = (f32[1024,2048]{1,0:T(8,128)S(1)}, f32[1024,2048]{1,0:T(8,128)}, u32[]{:S(2)}) copy-start(f32[1024,2048]{1,0:T(8,128)} %fusion.8) | copy-start | bytes 25165828
  21.0 2.7 %copy-start.3 = (bf16[2048,128]{1,0:T(8,128)(2,1)S(1)}, bf16[2048,128]{1,0:T(8,128)(2,1)}, u32[]{:S(2)}) copy-start(bf16[2048,128]{1,0:T(8,128)(2,1)} %param.7) | copy-start | bytes 1572868
  78.4 3.2 %collective-permute-start.2 = (f32[8,2048]{1,0:T(8,128)S(1)}, f32[8,2048]{1,0:T(8,128)S(1)}, u32[]{:S(2)}, u32[]{:S(2)}) collective-permute-start(f32[8,2048]{1,0:T(8,128)S(1)} %reduce_sum.39), channel_id=1, source_target_pairs={{0,16},{16,0},{32,48},{48,32},{64,80},{80,64},{96,112},{112,96},{1... | collective-permute-start | bytes 196616 | tf_op jit(solution)/shard_map/ppermute | solution.py:28
  81.6 4.8 %collective-permute-start.3 = (f32[8,2048]{1,0:T(8,128)S(1)}, f32[8,2048]{1,0:T(8,128)S(1)}, u32[]{:S(2)}, u32[]{:S(2)}) collective-permute-start(f32[8,2048]{1,0:T(8,128)S(1)} %add.41), channel_id=1, source_target_pairs={{0,32},{16,48},{32,0},{48,16},{64,96},{80,112},{96,64},{112,80},{1... | collective-permute-start | bytes 196616 | tf_op jit(solution)/shard_map/ppermute | solution.py:28
  86.4 7.3 %collective-permute-start.4 = (f32[8,2048]{1,0:T(8,128)S(1)}, f32[8,2048]{1,0:T(8,128)S(1)}, u32[]{:S(2)}, u32[]{:S(2)}) collective-permute-start(f32[8,2048]{1,0:T(8,128)S(1)} %add.42), channel_id=1, source_target_pairs={{0,64},{16,80},{32,96},{48,112},{64,0},{80,16},{96,32},{112,48},{1... | collective-permute-start | bytes 196616 | tf_op jit(solution)/shard_map/ppermute | solution.py:28
  93.7 4.7 %collective-permute-start.5 = (f32[8,2048]{1,0:T(8,128)S(1)}, f32[8,2048]{1,0:T(8,128)S(1)}, u32[]{:S(2)}, u32[]{:S(2)}) collective-permute-start(f32[8,2048]{1,0:T(8,128)S(1)} %add.43), channel_id=1, source_target_pairs={{0,128},{16,144},{32,160},{48,176},{64,192},{80,208},{96,224},{112... | collective-permute-start | bytes 196616 | tf_op jit(solution)/shard_map/ppermute | solution.py:28
  100.8 3.3 %collective-permute-start.6 = (f32[8,2048]{1,0:T(8,128)S(1)}, f32[8,2048]{1,0:T(8,128)S(1)}, u32[]{:S(2)}, u32[]{:S(2)}) collective-permute-start(f32[8,2048]{1,0:T(8,128)S(1)} %fusion), channel_id=1, source_target_pairs={{0,16},{16,0},{32,48},{48,32},{64,80},{80,64},{96,112},{112,96},{1... | collective-permute-start | bytes 196616 | tf_op jit(solution)/shard_map/ppermute | solution.py:28
  104.1 4.5 %collective-permute-start.7 = (f32[8,2048]{1,0:T(8,128)S(1)}, f32[8,2048]{1,0:T(8,128)S(1)}, u32[]{:S(2)}, u32[]{:S(2)}) collective-permute-start(f32[8,2048]{1,0:T(8,128)S(1)} %add.48), channel_id=1, source_target_pairs={{0,32},{16,48},{32,0},{48,16},{64,96},{80,112},{96,64},{112,80},{1... | collective-permute-start | bytes 196616 | tf_op jit(solution)/shard_map/ppermute | solution.py:28
  108.6 7.7 %collective-permute-start.8 = (f32[8,2048]{1,0:T(8,128)S(1)}, f32[8,2048]{1,0:T(8,128)S(1)}, u32[]{:S(2)}, u32[]{:S(2)}) collective-permute-start(f32[8,2048]{1,0:T(8,128)S(1)} %add.49), channel_id=1, source_target_pairs={{0,64},{16,80},{32,96},{48,112},{64,0},{80,16},{96,32},{112,48},{1... | collective-permute-start | bytes 196616 | tf_op jit(solution)/shard_map/ppermute | solution.py:28
  116.3 4.7 %collective-permute-start.9 = (f32[8,2048]{1,0:T(8,128)S(1)}, f32[8,2048]{1,0:T(8,128)S(1)}, u32[]{:S(2)}, u32[]{:S(2)}) collective-permute-start(f32[8,2048]{1,0:T(8,128)S(1)} %add.50), channel_id=1, source_target_pairs={{0,128},{16,144},{32,160},{48,176},{64,192},{80,208},{96,224},{112... | collective-permute-start | bytes 196616 | tf_op jit(solution)/shard_map/ppermute | solution.py:28
